TPU v7x, 32 devices: a whole 2x2x4 slice. The times are simulated.
32 devices in a mesh: dp: 8 (over y, x, core), expert: 4 (over z).
Axes of the slice: x: 2, y: 2, z: 4, core: 2. Of those that a mesh axis runs over, the one named last changes fastest.
Arguments:
- tokens: bfloat16 [4096, 1024], P(('dp', 'expert')), may hold values from -6 to 6
- expert_ids: int32 [4096, 2], P(('dp', 'expert')), may hold values from 0 to 3, all different within a row; in each aligned block of 128 rows (0 to 127, 128 to 255, ...) at most 96 rows name the same one
- routing: float32 [4096, 2], P(('dp', 'expert')), may hold values from 0.2 to 1
- w_gate: bfloat16 [4, 1024, 384], P('expert', 'dp'), may hold values from -0.1875 to 0.1875
- w_up: bfloat16 [4, 1024, 384], P('expert', 'dp'), may hold values from -0.1875 to 0.1875
- w_down: bfloat16 [4, 1024, 384], P('expert', 'dp'), may hold values from -0.3125 to 0.3125
- grad_out: bfloat16 [4096, 1024], P(('dp', 'expert')), may hold values from -6 to 6
Outputs:
- output: bfloat16 [4096, 1024], P(('dp', 'expert'))
- token_grad: bfloat16 [4096, 1024], P(('dp', 'expert'))
- down_grad: float32 [4, 1024, 384], P('expert', 'dp')
Inputs may be any that keep to these rules, and one draw needn't show every extreme that they name: `expert_ids`: the 2 experts of a token differ. Among the 128 tokens of one device no expert is named by more than 96 (token, choice) pairs, and in every draw some device names some expert exactly 96 times.
All inputs are finite; a program needn't handle non-finite values.
Results may differ from a plain program's by a relative error of at most 0.0065.
Values may be sent and summed in bfloat16 or wider, within the bound.
No kernel may reach another device: no remote copies, remote signals or barrier semaphores. Data moves between devices by JAX's collectives and lax.ppermute only.
A program may use at most 64 MiB of HBM per device.

v0:
```python
import jax
import jax.numpy as jnp
from jax import lax
from jax.sharding import PartitionSpec as P

contract_last = (((1,), (1,)), ((), ()))
contract_first = (((0,), (0,)), ((), ()))


def forward_rows(row_data, gate_w, up_w, down_w):
    gate_pre = jnp.dot(row_data, gate_w, preferred_element_type=jnp.float32)
    up_pre = jnp.dot(row_data, up_w, preferred_element_type=jnp.float32)
    sigmoid_val = jax.nn.sigmoid(gate_pre)
    hidden = (gate_pre * sigmoid_val * up_pre).astype(jnp.bfloat16)
    expert_out = lax.dot_general(
        hidden, down_w, contract_last, preferred_element_type=jnp.float32
    ).astype(jnp.bfloat16)
    return (gate_pre, up_pre, hidden, expert_out)


def backward_rows(grad_rows, gate_pre, up_pre, gate_w, up_w, down_w):
    hidden_grad = jnp.dot(grad_rows, down_w, preferred_element_type=jnp.float32)
    sigmoid_val = jax.nn.sigmoid(gate_pre)
    slope_val = sigmoid_val * (1.0 + gate_pre * (1.0 - sigmoid_val))
    gate_grad = (hidden_grad * up_pre * slope_val).astype(jnp.bfloat16)
    up_grad = (hidden_grad * gate_pre * sigmoid_val).astype(jnp.bfloat16)
    summed = lax.dot_general(gate_grad, gate_w, contract_last, preferred_element_type=jnp.float32)
    summed = summed + lax.dot_general(
        up_grad, up_w, contract_last, preferred_element_type=jnp.float32
    )
    return summed.astype(jnp.bfloat16)


def local(tokens, expert_ids, routing, w_gate, w_up, w_down, grad_out):
    tok_rows, width = tokens.shape
    groups = lax.axis_size("expert")
    local_count = w_gate.shape[0]
    ff_width = w_gate.shape[2]
    experts_all = local_count * groups
    top_count = expert_ids.shape[1]
    capacity = 3 * tok_rows * top_count // (2 * experts_all)
    pair_count = tok_rows * top_count
    chosen = expert_ids.reshape(pair_count)
    onehot = (chosen[:, None] == jnp.arange(experts_all, dtype=jnp.int32)[None, :]).astype(
        jnp.int32
    )
    before = jnp.cumsum(onehot, axis=0) - onehot
    slot_index = jnp.sum(before * onehot, axis=1)
    flat_index = chosen * capacity + slot_index
    owner_row = jnp.arange(pair_count, dtype=jnp.int32) // top_count
    slot_owner = (
        jnp.full((experts_all * capacity,), tok_rows, jnp.int32).at[flat_index].set(owner_row)
    )
    weight_slot = (
        jnp.zeros((experts_all * capacity,), jnp.float32)
        .at[flat_index]
        .set(routing.reshape(pair_count))
    )
    zero_row = jnp.zeros((1, width), jnp.bfloat16)
    send_rows = jnp.concatenate([tokens, zero_row], axis=0)[slot_owner].reshape(
        experts_all, capacity, width
    )
    grads_picked = jnp.concatenate([grad_out, zero_row], axis=0)[slot_owner].astype(jnp.float32)
    send_grads = (
        (weight_slot[:, None] * grads_picked)
        .astype(jnp.bfloat16)
        .reshape(experts_all, capacity, width)
    )
    shard_d = w_gate.shape[1]
    packed = jnp.concatenate([w_gate, w_up, w_down], axis=2)
    packed = jnp.transpose(packed, (1, 0, 2)).reshape(shard_d, local_count * 3 * ff_width)
    full = lax.all_gather(packed, "dp", axis=0, tiled=True)
    full = jnp.transpose(full.reshape(width, local_count, 3 * ff_width), (1, 0, 2))
    gate_full = full[:, :, :ff_width]
    up_full = full[:, :, ff_width : 2 * ff_width]
    down_full = full[:, :, 2 * ff_width :]
    recv_rows, recv_grads = (
        lax.all_to_all(send_rows, "expert", split_axis=0, concat_axis=0, tiled=True),
        lax.all_to_all(send_grads, "expert", split_axis=0, concat_axis=0, tiled=True),
    )
    rows_x = recv_rows.reshape(groups, local_count, capacity, width)
    rows_g = recv_grads.reshape(groups, local_count, capacity, width)
    slab_rows = groups * capacity
    expert_index = 0
    x_rows = rows_x[:, expert_index].reshape(slab_rows, width)
    g_rows = rows_g[:, expert_index].reshape(slab_rows, width)
    gate_w = gate_full[expert_index]
    up_w = up_full[expert_index]
    down_w = down_full[expert_index]
    is_valid = None
    position = None
    live_rows = None
    g_used = g_rows
    gate_pre, up_pre, hidden, expert_out = forward_rows(x_rows, gate_w, up_w, down_w)
    out_parts = [expert_out]
    forward_parts = [(gate_pre, up_pre, hidden, g_used, is_valid, position, live_rows)]
    out_send = jnp.stack(out_parts, axis=1).reshape(groups * local_count, capacity, width)
    back_out = lax.all_to_all(out_send, "expert", split_axis=0, concat_axis=0, tiled=True)
    expert_index = 0
    gate_pre, up_pre, hidden, g_used, is_valid, position, live_rows = forward_parts[expert_index]
    gate_w = gate_full[expert_index]
    up_w = up_full[expert_index]
    down_w = down_full[expert_index]
    grad_parts = [backward_rows(g_used, gate_pre, up_pre, gate_w, up_w, down_w)]
    grad_send = jnp.stack(grad_parts, axis=1).reshape(groups * local_count, capacity, width)
    back_grad = lax.all_to_all(grad_send, "expert", split_axis=0, concat_axis=0, tiled=True)
    out_rows = back_out.reshape(experts_all * capacity, width)[flat_index].reshape(
        tok_rows, top_count, width
    )
    output = jnp.sum(routing[:, :, None] * out_rows.astype(jnp.float32), axis=1).astype(
        jnp.bfloat16
    )
    grad_rows = back_grad.reshape(experts_all * capacity, width)[flat_index].reshape(
        tok_rows, top_count, width
    )
    token_grad = jnp.sum(grad_rows.astype(jnp.float32), axis=1).astype(jnp.bfloat16)
    shard_rows = w_gate.shape[1]
    saved = forward_parts[0]
    grad_cols = saved[3]
    pieces = lax.dot_general(
        grad_cols, saved[2], contract_first, preferred_element_type=jnp.float32
    )
    summed = lax.psum_scatter(pieces, "dp", scatter_dimension=0, tiled=True)
    down_grad = jnp.transpose(
        (summed / lax.axis_size("dp")).reshape(shard_rows, local_count, ff_width), (1, 0, 2)
    )
    return (output, token_grad, down_grad)


def solution(mesh):
    return jax.shard_map(
        local,
        mesh=mesh,
        in_specs=(
            P(("dp", "expert"), None),
            P(("dp", "expert"), None),
            P(("dp", "expert"), None),
            P("expert", "dp", None),
            P("expert", "dp", None),
            P("expert", "dp", None),
            P(("dp", "expert"), None),
        ),
        out_specs=(P(("dp", "expert"), None), P(("dp", "expert"), None), P("expert", "dp", None)),
        check_vma=False,
    )
```

profile of v0, /device:TPU:0, one launch (start us, length us, event | category | flops | bytes accessed | tf_op | source)
XLA Modules:
  0.0 127.7 jit_solution(5773724412011694440)
XLA Ops:
  7.2 1.7 %pad_maximum_fusion = bf16[1,128,1152]{2,1,0:T(8,128)(2,1)} fusion(bf16[1,128,384]{2,1,0:T(8,128)(2,1)} %param.12, bf16[1,128,384]{2,1,0:T(8,128)(2,1)} %param.11, bf16[1,128,384]{2,1,0:T(8,128)(2,1)} %param.10), kind=kLoop, calls=%fused_computation.22 | loop fusion | flops 884736 | bytes 589824 | tf_op jit(solution)/shard_map/concatenate | solution.py:70
  11.0 1.2 reduce-window.6
  13.6 1.4 %scatter_custom_fusion = s32[384]{0:T(512)S(1)} fusion(s32[256]{0:T(256)S(1)} %bitcast.61, s32[256]{0:T(256)S(1)} %and_select_fusion, s32[]{:T(128)} %constant.32.clone.1), kind=kCustom, calls=%fused_computation.43 | custom fusion | bytes 1540 | tf_op jit(solution)/shard_map/scatter | solution.py:52
  15.1 2.7 %gather_fusion = bf16[384,1024]{1,0:T(8,128)(2,1)} fusion(bf16[129,1024]{1,0:T(8,128)(2,1)S(1)} %concatenate.9, s32[1024]{0:T(1024)S(1)} %pad_clamp_fusion.1), kind=kCustom, calls=%fused_computation | custom fusion | bytes 1574400 | tf_op jit(solution)/shard_map/gather | solution.py:60
  17.8 6.3 %all-to-all-start = ((bf16[4,96,1024]{2,1,0:T(8,128)(2,1)}), bf16[4,96,1024]{2,1,0:T(8,128)(2,1)S(1)}, u32[]{:S(2)}, u32[]{:S(2)}) async-start(bf16[4,96,1024]{2,1,0:T(8,128)(2,1)} %bitcast.4), calls=%async_computation | async-start | bytes 1572864 | tf_op jit(solution)/shard_map/all_to_all | solution.py:78
  24.4 1.4 %scatter_custom_fusion.1 = f32[384]{0:T(512)S(1)} fusion(s32[256]{0:T(256)S(1)} %bitcast.62, f32[256]{0:T(256)S(1)} %reshape.133, f32[]{:T(128)} %constant.40.clone.1), kind=kCustom, calls=%fused_computation.41 | custom fusion | bytes 1540 | tf_op jit(solution)/shard_map/scatter | solution.py:57
  25.9 2.1 %gather_fusion.2 = bf16[384,1024]{1,0:T(8,128)(2,1)S(1)} fusion(bf16[129,1024]{1,0:T(8,128)(2,1)S(1)} %concatenate.11, s32[1024]{0:T(1024)S(1)} %pad_clamp_fusion.1), kind=kCustom, calls=%fused_computation.2 | custom fusion | bytes 1574400 | tf_op jit(solution)/shard_map/gather | solution.py:63
  29.0 15.2 %all-to-all-done = bf16[4,96,1024]{2,1,0:T(8,128)(2,1)S(1)} async-done(((bf16[4,96,1024]{2,1,0:T(8,128)(2,1)}), bf16[4,96,1024]{2,1,0:T(8,128)(2,1)S(1)}, u32[]{:S(2)}, u32[]{:S(2)}) %all-to-all-start) | async-done | bytes 786464 | tf_op jit(solution)/shard_map/all_to_all | solution.py:78
  44.2 3.5 %all-to-all-start.2 = ((bf16[4,96,1024]{2,1,0:T(8,128)(2,1)}), bf16[4,96,1024]{2,1,0:T(8,128)(2,1)S(1)}, u32[]{:S(2)}, u32[]{:S(2)}) async-start(bf16[4,96,1024]{2,1,0:T(8,128)(2,1)} %fusion), calls=%async_computation.2 | async-start | bytes 1572864 | tf_op jit(solution)/shard_map/all_to_all | solution.py:79
  47.7 1.7 %fusion.2 = f32[384,384]{1,0:T(8,128)S(1)} fusion(bf16[384,1024]{1,0:T(8,128)(2,1)S(1)} %bitcast.59, bf16[1,1024,1152]{2,1,0:T(8,128)(2,1)} %all-gather.3.cloned.1.call-done), kind=kOutput, calls=%fused_computation.15 | convolution fusion | flops 301989888 | bytes 2162688 | tf_op jit(solution)/shard_map/dot_general | solution.py:11
  49.4 1.7 %multiply_convert_fusion.2 = (bf16[384,384]{1,0:T(8,128)(2,1)S(1)}, f32[384,384]{1,0:T(8,128)S(1)}) fusion(f32[384,384]{1,0:T(8,128)S(1)} %fusion.2, bf16[384,1024]{1,0:T(8,128)(2,1)S(1)} %bitcast.60, bf16[1,1024,1152]{2,1,0:T(8,128)(2,1)} %all-gather.3.cloned.1.call-done), kind=kOutput, calls=%fused_computation.20 | convolution fusion | flops 302874624 | bytes 3047424 | tf_op jit(solution)/shard_map/dot_general | solution.py:12
  51.2 2.6 %convolution_convert_fusion = bf16[384,1024]{1,0:T(8,128)(2,1)} fusion(bf16[384,384]{1,0:T(8,128)(2,1)S(1)} %get-tuple-element.3, bf16[1,1024,1152]{2,1,0:T(8,128)(2,1)} %all-gather.3.cloned.1.call-done), kind=kOutput, calls=%fused_computation.9 | convolution fusion | flops 302383104 | bytes 1867776 | tf_op jit(solution)/shard_map/dot_general | solution.py:15
  53.8 13.6 %all-to-all-done.2 = bf16[4,96,1024]{2,1,0:T(8,128)(2,1)S(1)} async-done(((bf16[4,96,1024]{2,1,0:T(8,128)(2,1)}), bf16[4,96,1024]{2,1,0:T(8,128)(2,1)S(1)}, u32[]{:S(2)}, u32[]{:S(2)}) %all-to-all-start.2) | async-done | bytes 786464 | tf_op jit(solution)/shard_map/all_to_all | solution.py:79
  67.3 3.5 %all-to-all-start.1 = ((bf16[4,96,1024]{2,1,0:T(8,128)(2,1)}), bf16[4,96,1024]{2,1,0:T(8,128)(2,1)S(1)}, u32[]{:S(2)}, u32[]{:S(2)}) async-start(bf16[4,96,1024]{2,1,0:T(8,128)(2,1)} %bitcast.9), calls=%async_computation.1 | async-start | bytes 1572864 | tf_op jit(solution)/shard_map/all_to_all | solution.py:98
  70.9 1.9 %fusion.16 = f32[1024,384]{1,0:T(8,128)} fusion(bf16[384,1024]{1,0:T(8,128)(2,1)S(1)} %bitcast.56, bf16[384,384]{1,0:T(8,128)(2,1)S(1)} %get-tuple-element.3), kind=kOutput, calls=%fused_computation.48 | convolution fusion | flops 301989888 | bytes 2654208 | tf_op jit(solution)/shard_map/dot_general | solution.py:120
  72.8 1.7 %fusion.4 = f32[384,384]{1,0:T(8,128)S(1)} fusion(bf16[384,1024]{1,0:T(8,128)(2,1)S(1)} %bitcast.57, bf16[1,1024,1152]{2,1,0:T(8,128)(2,1)} %all-gather.3.cloned.1.call-done), kind=kOutput, calls=%fused_computation.17 | convolution fusion | flops 301989888 | bytes 2162688 | tf_op jit(solution)/shard_map/dot_general | solution.py:22
  74.5 1.8 %fusion.1 = f32[384,1024]{1,0:T(8,128)S(1)} fusion(bf16[1,1024,1152]{2,1,0:T(8,128)(2,1)} %all-gather.3.cloned.1.call-done, f32[384,384]{1,0:T(8,128)S(1)} %fusion.2, f32[384,384]{1,0:T(8,128)S(1)} %fusion.4, f32[384,384]{1,0:T(8,128)S(1)} %get-tuple-element.4), kind=kOutput, calls=%fused_computation.14 | convolution fusion | flops 303464448 | bytes 4128768 | tf_op jit(solution)/shard_map/dot_general | solution.py:27
  76.3 2.7 %add_convert_fusion = bf16[384,1024]{1,0:T(8,128)(2,1)} fusion(f32[384,1024]{1,0:T(8,128)S(1)} %fusion.1, bf16[1,1024,1152]{2,1,0:T(8,128)(2,1)} %all-gather.3.cloned.1.call-done, f32[384,384]{1,0:T(8,128)S(1)} %fusion.4, f32[384,384]{1,0:T(8,128)S(1)} %fusion.2), kind=kOutput, calls=%fused_computation.8 | convolution fusion | flops 303661056 | bytes 4325376 | tf_op jit(solution)/shard_map/dot_general | solution.py:28
  79.0 11.5 %all-to-all-done.1 = bf16[4,96,1024]{2,1,0:T(8,128)(2,1)S(1)} async-done(((bf16[4,96,1024]{2,1,0:T(8,128)(2,1)}), bf16[4,96,1024]{2,1,0:T(8,128)(2,1)S(1)}, u32[]{:S(2)}, u32[]{:S(2)}) %all-to-all-start.1) | async-done | bytes 786464 | tf_op jit(solution)/shard_map/all_to_all | solution.py:98
  90.5 3.7 %all-to-all-start.3 = ((bf16[4,96,1024]{2,1,0:T(8,128)(2,1)}), bf16[4,96,1024]{2,1,0:T(8,128)(2,1)S(1)}, u32[]{:S(2)}, u32[]{:S(2)}) async-start(bf16[4,96,1024]{2,1,0:T(8,128)(2,1)} %bitcast.13), calls=%async_computation.3 | async-start | bytes 1572864 | tf_op jit(solution)/shard_map/all_to_all | solution.py:106
  96.0 17.6 %all-to-all-done.3 = bf16[4,96,1024]{2,1,0:T(8,128)(2,1)S(1)} async-done(((bf16[4,96,1024]{2,1,0:T(8,128)(2,1)}), bf16[4,96,1024]{2,1,0:T(8,128)(2,1)S(1)}, u32[]{:S(2)}, u32[]{:S(2)}) %all-to-all-start.3) | async-done | bytes 786464 | tf_op jit(solution)/shard_map/all_to_all | solution.py:106
  115.0 2.1 %reduce_sum.35 = bf16[128,1024]{1,0:T(8,128)(2,1)} reduce(bf16[128,2,1024]{2,1,0:T(2,128)(2,1)S(1)} %reshape.86, bf16[]{:T(256)} %constant.16.clone.1), dimensions={1}, to_apply=%region_6.7 | reduce | flops 131072 | bytes 786434 | tf_op jit(solution)/shard_map/reduce_sum | solution.py:116
  117.1 2.1 %multiply_reduce_fusion = bf16[128,1024]{1,0:T(8,128)(2,1)} fusion(f32[128,2,1024]{2,1,0:T(2,128)S(1)} %reshape.87, f32[128,2]{1,0:T(8,128)S(1)} %copy.13), kind=kLoop, calls=%fused_computation.10 | loop fusion | flops 393216 | bytes 1311744 | tf_op jit(solution)/shard_map/reduce_sum | solution.py:110
  119.2 1.6 %multiply_bitcast_fusion = f32[1,128,384]{2,1,0:T(8,128)} fusion(f32[128,384]{1,0:T(8,128)} %reduce-scatter.2.cloned.1.call-done), kind=kLoop, calls=%fused_computation.25 | loop fusion | flops 49152 | bytes 393216 | tf_op jit(solution)/shard_map/transpose;reshape | solution.py:124
  (39 shorter events, 8.2 us)
Async XLA Ops:
  7.2 40.6 %all-gather.3.cloned.1.call-start = ((), (), s32[]{:S(2)}) async-start(), calls=%async_computation.6 | async-start | bytes 2654208 | tf_op jit(solution)/shard_map/all_gather | solution.py:72
  15.0 9.1 %copy-start.1 = (f32[128,2]{0,1:T(2,128)S(1)}, f32[128,2]{0,1:T(2,128)}, u32[]{:S(2)}) copy-start(f32[128,2]{0,1:T(2,128)} %param.9) | copy-start | bytes 3076
  15.1 10.8 %copy-start = (bf16[128,1024]{1,0:T(8,128)(2,1)S(1)}, bf16[128,1024]{1,0:T(8,128)(2,1)}, u32[]{:S(2)}) copy-start(bf16[128,1024]{1,0:T(8,128)(2,1)} %param.13) | copy-start | bytes 786436
  17.8 26.5 %all-to-all-start = ((bf16[4,96,1024]{2,1,0:T(8,128)(2,1)}), bf16[4,96,1024]{2,1,0:T(8,128)(2,1)S(1)}, u32[]{:S(2)}, u32[]{:S(2)}) async-start(bf16[4,96,1024]{2,1,0:T(8,128)(2,1)} %bitcast.4), calls=%async_computation | async-start | bytes 1572864 | tf_op jit(solution)/shard_map/all_to_all | solution.py:78
  44.2 23.1 %all-to-all-start.2 = ((bf16[4,96,1024]{2,1,0:T(8,128)(2,1)}), bf16[4,96,1024]{2,1,0:T(8,128)(2,1)S(1)}, u32[]{:S(2)}, u32[]{:S(2)}) async-start(bf16[4,96,1024]{2,1,0:T(8,128)(2,1)} %fusion), calls=%async_computation.2 | async-start | bytes 1572864 | tf_op jit(solution)/shard_map/all_to_all | solution.py:79
  67.3 23.1 %all-to-all-start.1 = ((bf16[4,96,1024]{2,1,0:T(8,128)(2,1)}), bf16[4,96,1024]{2,1,0:T(8,128)(2,1)S(1)}, u32[]{:S(2)}, u32[]{:S(2)}) async-start(bf16[4,96,1024]{2,1,0:T(8,128)(2,1)} %bitcast.9), calls=%async_computation.1 | async-start | bytes 1572864 | tf_op jit(solution)/shard_map/all_to_all | solution.py:98
  70.8 48.4 %reduce-scatter.2.cloned.1.call-start = ((), (), s32[]{:S(2)}) async-start(), calls=%async_computation.5 | async-start | bytes 1769472 | tf_op jit(solution)/shard_map/reduce_scatter | solution.py:123
  90.5 23.1 %all-to-all-start.3 = ((bf16[4,96,1024]{2,1,0:T(8,128)(2,1)}), bf16[4,96,1024]{2,1,0:T(8,128)(2,1)S(1)}, u32[]{:S(2)}, u32[]{:S(2)}) async-start(bf16[4,96,1024]{2,1,0:T(8,128)(2,1)} %bitcast.13), calls=%async_computation.3 | async-start | bytes 1572864 | tf_op jit(solution)/shard_map/all_to_all | solution.py:106
Sparse Core Ops, SparseCore 0:
  9.9 31.6 all-gather.2
  75.0 39.7 reduce-scatter.1
where the time goes:
time: 128 us
  waiting for transfers between devices  57.9 us (45%)
  starting transfers between devices  17.1 us (13%)
  between operations  14.2 us (11%)
  matrix products  14.1 us (11%)
  local copies, waits for them, and re-layouts  13.7 us (11%)
  other arithmetic  10.7 us (8%)
    all_to_all x1, waiting for transfers between devices, local(): lax.all_to_all(grad_send, 'expert', split_axis=0, concat_axis=0, tiled=True)  17.6 us
    all_to_all x1, waiting for transfers between devices, local(): lax.all_to_all(send_rows, 'expert', split_axis=0, concat_axis=0, tiled=True)  15.2 us
    all_to_all x1, waiting for transfers between devices, local(): lax.all_to_all(send_grads, 'expert', split_axis=0, concat_axis=0, tiled=T...  13.6 us
    all_to_all x1, waiting for transfers between devices, local(): lax.all_to_all(out_send, 'expert', split_axis=0, concat_axis=0, tiled=True)  11.5 us
    all_to_all x1, starting transfers between devices, local(): lax.all_to_all(send_rows, 'expert', split_axis=0, concat_axis=0, tiled=True)  6.35 us
    all_to_all x1, starting transfers between devices, local(): lax.all_to_all(grad_send, 'expert', split_axis=0, concat_axis=0, tiled=True)  3.67 us
    all_to_all x1, starting transfers between devices, local(): lax.all_to_all(send_grads, 'expert', split_axis=0, concat_axis=0, tiled=T...  3.49 us
    all_to_all x1, starting transfers between devices, local(): lax.all_to_all(out_send, 'expert', split_axis=0, concat_axis=0, tiled=True)  3.49 us
  transfers between devices with their start and end apart: 6, of which 4 were waited for; matrix products, arithmetic and copies ran while one was open for 27% of the time, Pallas kernels for 0%

commit v1 on v0

--- a/solution.py
+++ b/solution.py
@@ -5,6 +5,22 @@
 
 contract_last = (((1,), (1,)), ((), ()))
 contract_first = (((0,), (0,)), ((), ()))
+
+
+def pairwise_exchange(x, axis, split, join):
+    ways, here = (lax.axis_size(axis), lax.axis_index(axis))
+    width = x.shape[split] // ways
+    lengths = list(x.shape)
+    lengths[split] = width
+    height = lengths[join]
+    lengths[join] = height * ways
+    full = jnp.zeros(lengths, x.dtype)
+    for mask in range(ways):
+        part = lax.dynamic_slice_in_dim(x, (here ^ mask) * width, width, axis=split)
+        if mask:
+            part = lax.ppermute(part, axis, [(d, d ^ mask) for d in range(ways)])
+        full = lax.dynamic_update_slice_in_dim(full, part, (here ^ mask) * height, axis=join)
+    return full
 
 
 def forward_rows(row_data, gate_w, up_w, down_w):
@@ -103,7 +119,7 @@
     down_w = down_full[expert_index]
     grad_parts = [backward_rows(g_used, gate_pre, up_pre, gate_w, up_w, down_w)]
     grad_send = jnp.stack(grad_parts, axis=1).reshape(groups * local_count, capacity, width)
-    back_grad = lax.all_to_all(grad_send, "expert", split_axis=0, concat_axis=0, tiled=True)
+    back_grad = pairwise_exchange(grad_send, "expert", 0, 0)
     out_rows = back_out.reshape(experts_all * capacity, width)[flat_index].reshape(
         tok_rows, top_count, width
     )

time: 128 us -> 126 us (0.984)
  waiting for transfers between devices: 57.9 us -> 54.4 us
    ppermute x0 -> x3, waiting for transfers between devices: none -> 23 us  [pairwise_exchange(): part = lax.ppermute(part, axis, [(d, d ^ mask) for d in range(ways)])]
    all_to_all x1 -> x0, waiting for transfers between devices: 17.6 us -> none  [local(): lax.all_to_all(grad_send, 'expert', split_axis=0, concat_axis=0, tiled=True)]
    all_to_all x1, waiting for transfers between devices: 11.5 us -> 0.01 us  [local(): lax.all_to_all(out_send, 'expert', split_axis=0, concat_axis=0, tiled=True)]
    ppermute x0 -> x3, starting transfers between devices: none -> 4.45 us  [pairwise_exchange(): part = lax.ppermute(part, axis, [(d, d ^ mask) for d in range(ways)])]
    all_to_all x1 -> x0, starting transfers between devices: 3.67 us -> none  [local(): lax.all_to_all(grad_send, 'expert', split_axis=0, concat_axis=0, tiled=True)]
    all_to_all x1, waiting for transfers between devices: 13.6 us -> 16.1 us  [local(): lax.all_to_all(send_grads, 'expert', split_axis=0, concat_axis=0, tiled=T...]
  transfers between devices with their start and end apart: 6 -> 8, of which waited for: 4 -> 4; matrix products, arithmetic and copies ran while one was open for 27% -> 26% of each run, Pallas kernels for 0% -> 0%
where the time goes in v1:
time: 126 us; the launch traced here: 125 us
  waiting for transfers between devices  54.4 us (43%)
  starting transfers between devices  18 us (14%)
  between operations  14.3 us (11%)
  local copies, waits for them, and re-layouts  13.9 us (11%)
  matrix products  13.3 us (11%)
  other arithmetic  10.7 us (8%)
    ppermute x3, waiting for transfers between devices, pairwise_exchange(): part = lax.ppermute(part, axis, [(d, d ^ mask) for d in range(ways)])  23 us
    all_to_all x1, waiting for transfers between devices, local(): lax.all_to_all(send_grads, 'expert', split_axis=0, concat_axis=0, tiled=T...  16.1 us
    all_to_all x1, waiting for transfers between devices, local(): lax.all_to_all(send_rows, 'expert', split_axis=0, concat_axis=0, tiled=True)  15.1 us
    all_to_all x1, starting transfers between devices, local(): lax.all_to_all(send_rows, 'expert', split_axis=0, concat_axis=0, tiled=True)  6.35 us
    ppermute x3, starting transfers between devices, pairwise_exchange(): part = lax.ppermute(part, axis, [(d, d ^ mask) for d in range(ways)])  4.45 us
    all_to_all x1, starting transfers between devices, local(): lax.all_to_all(out_send, 'expert', split_axis=0, concat_axis=0, tiled=True)  3.67 us
    all_to_all x1, starting transfers between devices, local(): lax.all_to_all(send_grads, 'expert', split_axis=0, concat_axis=0, tiled=T...  3.49 us
    gather x1, local copies, waits for them, and re-layouts, local(): jnp.concatenate([tokens, zero_row], axis=0)[slot_owner]  2.68 us
  transfers between devices with their start and end apart: 8, of which 4 were waited for; matrix products, arithmetic and copies ran while one was open for 26% of the time, Pallas kernels for 0%

profile of v1, /device:TPU:0, one launch (start us, length us, event | category | flops | bytes accessed | tf_op | source)
XLA Modules:
  0.0 124.6 jit_solution(18045329835678423451)
XLA Ops:
  7.2 1.7 %pad_maximum_fusion = bf16[1,128,1152]{2,1,0:T(8,128)(2,1)} fusion(bf16[1,128,384]{2,1,0:T(8,128)(2,1)} %param.12, bf16[1,128,384]{2,1,0:T(8,128)(2,1)} %param.11, bf16[1,128,384]{2,1,0:T(8,128)(2,1)} %param.10), kind=kLoop, calls=%fused_computation.22 | loop fusion | flops 884736 | bytes 589824 | tf_op jit(solution)/shard_map/concatenate | solution.py:86
  13.6 1.4 %scatter_custom_fusion = s32[384]{0:T(512)S(1)} fusion(s32[256]{0:T(256)S(1)} %bitcast.60, s32[256]{0:T(256)S(1)} %and_select_fusion, s32[]{:T(128)} %constant.17.clone.1), kind=kCustom, calls=%fused_computation.50 | custom fusion | bytes 1540 | tf_op jit(solution)/shard_map/scatter | solution.py:68
  15.1 2.7 %gather_fusion = bf16[384,1024]{1,0:T(8,128)(2,1)} fusion(bf16[129,1024]{1,0:T(8,128)(2,1)S(1)} %concatenate.9, s32[1024]{0:T(1024)S(1)} %pad_clamp_fusion.1), kind=kCustom, calls=%fused_computation | custom fusion | bytes 1574400 | tf_op jit(solution)/shard_map/gather | solution.py:76
  17.7 6.3 %all-to-all-start = ((bf16[4,96,1024]{2,1,0:T(8,128)(2,1)}), bf16[4,96,1024]{2,1,0:T(8,128)(2,1)S(1)}, u32[]{:S(2)}, u32[]{:S(2)}) async-start(bf16[4,96,1024]{2,1,0:T(8,128)(2,1)} %bitcast.4), calls=%async_computation | async-start | bytes 1572864 | tf_op jit(solution)/shard_map/all_to_all | solution.py:94
  24.1 2.1 %gather_fusion.2 = bf16[384,1024]{1,0:T(8,128)(2,1)S(1)} fusion(bf16[129,1024]{1,0:T(8,128)(2,1)S(1)} %concatenate.11, s32[1024]{0:T(1024)S(1)} %pad_clamp_fusion.1), kind=kCustom, calls=%fused_computation.2 | custom fusion | bytes 1574400 | tf_op jit(solution)/shard_map/gather | solution.py:79
  26.5 1.4 %scatter_custom_fusion.1 = f32[384]{0:T(512)S(1)} fusion(s32[256]{0:T(256)S(1)} %bitcast.61, f32[256]{0:T(256)S(1)} %reshape.133, f32[]{:T(128)} %constant.47.clone.1), kind=kCustom, calls=%fused_computation.48 | custom fusion | bytes 1540 | tf_op jit(solution)/shard_map/scatter | solution.py:73
  29.1 15.1 %all-to-all-done = bf16[4,96,1024]{2,1,0:T(8,128)(2,1)S(1)} async-done(((bf16[4,96,1024]{2,1,0:T(8,128)(2,1)}), bf16[4,96,1024]{2,1,0:T(8,128)(2,1)S(1)}, u32[]{:S(2)}, u32[]{:S(2)}) %all-to-all-start) | async-done | bytes 786464 | tf_op jit(solution)/shard_map/all_to_all | solution.py:94
  44.2 3.5 %all-to-all-start.2 = ((bf16[4,96,1024]{2,1,0:T(8,128)(2,1)}), bf16[4,96,1024]{2,1,0:T(8,128)(2,1)S(1)}, u32[]{:S(2)}, u32[]{:S(2)}) async-start(bf16[4,96,1024]{2,1,0:T(8,128)(2,1)} %fusion), calls=%async_computation.2 | async-start | bytes 1572864 | tf_op jit(solution)/shard_map/all_to_all | solution.py:95
  47.8 1.7 %fusion.2 = f32[384,384]{1,0:T(8,128)S(1)} fusion(bf16[384,1024]{1,0:T(8,128)(2,1)S(1)} %bitcast.57, bf16[1,1024,1152]{2,1,0:T(8,128)(2,1)} %all-gather.3.cloned.1.call-done), kind=kOutput, calls=%fused_computation.15 | convolution fusion | flops 301989888 | bytes 2162688 | tf_op jit(solution)/shard_map/dot_general | solution.py:27
  49.5 1.7 %multiply_convert_fusion.2 = (bf16[384,384]{1,0:T(8,128)(2,1)S(1)}, f32[384,384]{1,0:T(8,128)S(1)}) fusion(f32[384,384]{1,0:T(8,128)S(1)} %fusion.2, bf16[384,1024]{1,0:T(8,128)(2,1)S(1)} %bitcast.58, bf16[1,1024,1152]{2,1,0:T(8,128)(2,1)} %all-gather.3.cloned.1.call-done), kind=kOutput, calls=%fused_computation.20 | convolution fusion | flops 302874624 | bytes 3047424 | tf_op jit(solution)/shard_map/dot_general | solution.py:28
  51.2 16.1 %all-to-all-done.2 = bf16[4,96,1024]{2,1,0:T(8,128)(2,1)S(1)} async-done(((bf16[4,96,1024]{2,1,0:T(8,128)(2,1)}), bf16[4,96,1024]{2,1,0:T(8,128)(2,1)S(1)}, u32[]{:S(2)}, u32[]{:S(2)}) %all-to-all-start.2) | async-done | bytes 786464 | tf_op jit(solution)/shard_map/all_to_all | solution.py:95
  67.3 1.9 %fusion.16 = f32[1024,384]{1,0:T(8,128)} fusion(bf16[384,1024]{1,0:T(8,128)(2,1)S(1)} %bitcast.54, bf16[384,384]{1,0:T(8,128)(2,1)S(1)} %get-tuple-element.7), kind=kOutput, calls=%fused_computation.55 | convolution fusion | flops 301989888 | bytes 2654208 | tf_op jit(solution)/shard_map/dot_general | solution.py:136
  69.2 2.6 %convolution_convert_fusion = bf16[384,1024]{1,0:T(8,128)(2,1)} fusion(bf16[384,384]{1,0:T(8,128)(2,1)S(1)} %get-tuple-element.7, bf16[1,1024,1152]{2,1,0:T(8,128)(2,1)} %all-gather.3.cloned.1.call-done), kind=kOutput, calls=%fused_computation.9 | convolution fusion | flops 302383104 | bytes 1867776 | tf_op jit(solution)/shard_map/dot_general | solution.py:31
  71.8 3.7 %all-to-all-start.1 = ((bf16[4,96,1024]{2,1,0:T(8,128)(2,1)}), bf16[4,96,1024]{2,1,0:T(8,128)(2,1)S(1)}, u32[]{:S(2)}, u32[]{:S(2)}) async-start(bf16[4,96,1024]{2,1,0:T(8,128)(2,1)} %bitcast.9), calls=%async_computation.1 | async-start | bytes 1572864 | tf_op jit(solution)/shard_map/all_to_all | solution.py:114
  75.5 1.7 %fusion.4 = f32[384,384]{1,0:T(8,128)S(1)} fusion(bf16[384,1024]{1,0:T(8,128)(2,1)S(1)} %bitcast.55, bf16[1,1024,1152]{2,1,0:T(8,128)(2,1)} %all-gather.3.cloned.1.call-done), kind=kOutput, calls=%fused_computation.17 | convolution fusion | flops 301989888 | bytes 2162688 | tf_op jit(solution)/shard_map/dot_general | solution.py:38
  77.3 1.8 %fusion.1 = f32[384,1024]{1,0:T(8,128)S(1)} fusion(bf16[1,1024,1152]{2,1,0:T(8,128)(2,1)} %all-gather.3.cloned.1.call-done, f32[384,384]{1,0:T(8,128)S(1)} %fusion.2, f32[384,384]{1,0:T(8,128)S(1)} %fusion.4, f32[384,384]{1,0:T(8,128)S(1)} %get-tuple-element.8), kind=kOutput, calls=%fused_computation.14 | convolution fusion | flops 303464448 | bytes 4128768 | tf_op jit(solution)/shard_map/dot_general | solution.py:43
  79.1 1.8 %add_convert_fusion = bf16[384,1024]{1,0:T(8,128)(2,1)S(1)} fusion(f32[384,1024]{1,0:T(8,128)S(1)} %fusion.1, bf16[1,1024,1152]{2,1,0:T(8,128)(2,1)} %all-gather.3.cloned.1.call-done, f32[384,384]{1,0:T(8,128)S(1)} %fusion.4, f32[384,384]{1,0:T(8,128)S(1)} %fusion.2), kind=kOutput, calls=%fused_computation.8 | convolution fusion | flops 303661056 | bytes 4325376 | tf_op jit(solution)/shard_map/dot_general | solution.py:44
  81.1 1.9 %collective-permute-start = (bf16[1,96,1024]{2,1,0:T(8,128)(2,1)S(1)}, bf16[1,96,1024]{2,1,0:T(8,128)(2,1)S(1)}, u32[]{:S(2)}, u32[]{:S(2)}) collective-permute-start(bf16[1,96,1024]{2,1,0:T(8,128)(2,1)S(1)} %get-tuple-element.5), channel_id=1, source_target_pairs={{0,1},{1,0},{2,3},{3,2},{4,5},{5,4},{6,7},{7,6},{8,9},{9,8},{10,11... | collective-permute-start | bytes 589832 | tf_op jit(solution)/shard_map/ppermute | solution.py:21
  83.0 2.4 %collective-permute-start.1 = (bf16[1,96,1024]{2,1,0:T(8,128)(2,1)S(1)}, bf16[1,96,1024]{2,1,0:T(8,128)(2,1)S(1)}, u32[]{:S(2)}, u32[]{:S(2)}) collective-permute-start(bf16[1,96,1024]{2,1,0:T(8,128)(2,1)S(1)} %get-tuple-element.4), channel_id=1, source_target_pairs={{0,2},{1,3},{2,0},{3,1},{4,6},{5,7},{6,4},{7,5},{8,10},{9,11},{10,... | collective-permute-start | bytes 589832 | tf_op jit(solution)/shard_map/ppermute | solution.py:21
  85.6 8.1 %collective-permute-done = bf16[1,96,1024]{2,1,0:T(8,128)(2,1)S(1)} collective-permute-done((bf16[1,96,1024]{2,1,0:T(8,128)(2,1)S(1)}, bf16[1,96,1024]{2,1,0:T(8,128)(2,1)S(1)}, u32[]{:S(2)}, u32[]{:S(2)}) %collective-permute-start) | collective-permute-done | bytes 196640 | tf_op jit(solution)/shard_map/ppermute | solution.py:21
  93.7 14.9 %collective-permute-done.1 = bf16[1,96,1024]{2,1,0:T(8,128)(2,1)S(1)} collective-permute-done((bf16[1,96,1024]{2,1,0:T(8,128)(2,1)S(1)}, bf16[1,96,1024]{2,1,0:T(8,128)(2,1)S(1)}, u32[]{:S(2)}, u32[]{:S(2)}) %collective-permute-start.1) | collective-permute-done | bytes 196640 | tf_op jit(solution)/shard_map/ppermute | solution.py:21
  110.1 2.1 %reduce_sum.35 = bf16[128,1024]{1,0:T(8,128)(2,1)} reduce(bf16[128,2,1024]{2,1,0:T(2,128)(2,1)S(1)} %reshape.86, bf16[]{:T(256)} %constant.16.clone.1), dimensions={1}, to_apply=%region_6.7 | reduce | flops 131072 | bytes 786434 | tf_op jit(solution)/shard_map/reduce_sum | solution.py:132
  114.0 2.1 %multiply_reduce_fusion = bf16[128,1024]{1,0:T(8,128)(2,1)} fusion(f32[128,2,1024]{2,1,0:T(2,128)S(1)} %reshape.87, f32[128,2]{1,0:T(8,128)S(1)} %copy.13), kind=kLoop, calls=%fused_computation.10 | loop fusion | flops 393216 | bytes 1311744 | tf_op jit(solution)/shard_map/reduce_sum | solution.py:126
  116.1 1.6 %multiply_bitcast_fusion = f32[1,128,384]{2,1,0:T(8,128)} fusion(f32[128,384]{1,0:T(8,128)} %reduce-scatter.2.cloned.1.call-done), kind=kLoop, calls=%fused_computation.26 | loop fusion | flops 49152 | bytes 393216 | tf_op jit(solution)/shard_map/transpose;reshape | solution.py:140
  (48 shorter events, 9.8 us)
Async XLA Ops:
  7.2 40.6 %all-gather.3.cloned.1.call-start = ((), (), s32[]{:S(2)}) async-start(), calls=%async_computation.5 | async-start | bytes 2654208 | tf_op jit(solution)/shard_map/all_gather | solution.py:88
  15.0 9.0 %copy-start = (bf16[128,1024]{1,0:T(8,128)(2,1)S(1)}, bf16[128,1024]{1,0:T(8,128)(2,1)}, u32[]{:S(2)}) copy-start(bf16[128,1024]{1,0:T(8,128)(2,1)} %param.13) | copy-start | bytes 786436
  17.7 26.5 %all-to-all-start = ((bf16[4,96,1024]{2,1,0:T(8,128)(2,1)}), bf16[4,96,1024]{2,1,0:T(8,128)(2,1)S(1)}, u32[]{:S(2)}, u32[]{:S(2)}) async-start(bf16[4,96,1024]{2,1,0:T(8,128)(2,1)} %bitcast.4), calls=%async_computation | async-start | bytes 1572864 | tf_op jit(solution)/shard_map/all_to_all | solution.py:94
  24.1 2.1 %copy-start.1 = (f32[128,2]{0,1:T(2,128)S(1)}, f32[128,2]{0,1:T(2,128)}, u32[]{:S(2)}) copy-start(f32[128,2]{0,1:T(2,128)} %param.9) | copy-start | bytes 3076
  44.2 23.1 %all-to-all-start.2 = ((bf16[4,96,1024]{2,1,0:T(8,128)(2,1)}), bf16[4,96,1024]{2,1,0:T(8,128)(2,1)S(1)}, u32[]{:S(2)}, u32[]{:S(2)}) async-start(bf16[4,96,1024]{2,1,0:T(8,128)(2,1)} %fusion), calls=%async_computation.2 | async-start | bytes 1572864 | tf_op jit(solution)/shard_map/all_to_all | solution.py:95
  47.7 68.4 %reduce-scatter.2.cloned.1.call-start = ((), (), s32[]{:S(2)}) async-start(), calls=%async_computation.4 | async-start | bytes 1769472 | tf_op jit(solution)/shard_map/reduce_scatter | solution.py:139
  71.8 40.4 %all-to-all-start.1 = ((bf16[4,96,1024]{2,1,0:T(8,128)(2,1)}), bf16[4,96,1024]{2,1,0:T(8,128)(2,1)S(1)}, u32[]{:S(2)}, u32[]{:S(2)}) async-start(bf16[4,96,1024]{2,1,0:T(8,128)(2,1)} %bitcast.9), calls=%async_computation.1 | async-start | bytes 1572864 | tf_op jit(solution)/shard_map/all_to_all | solution.py:114
  81.1 12.6 %collective-permute-start = (bf16[1,96,1024]{2,1,0:T(8,128)(2,1)S(1)}, bf16[1,96,1024]{2,1,0:T(8,128)(2,1)S(1)}, u32[]{:S(2)}, u32[]{:S(2)}) collective-permute-start(bf16[1,96,1024]{2,1,0:T(8,128)(2,1)S(1)} %get-tuple-element.5), channel_id=1, source_target_pairs={{0,1},{1,0},{2,3},{3,2},{4,5},{5,4},{6,7},{7,6},{8,9},{9,8},{10,11... | collective-permute-start | bytes 589832 | tf_op jit(solution)/shard_map/ppermute | solution.py:21
  83.0 25.6 %collective-permute-start.1 = (bf16[1,96,1024]{2,1,0:T(8,128)(2,1)S(1)}, bf16[1,96,1024]{2,1,0:T(8,128)(2,1)S(1)}, u32[]{:S(2)}, u32[]{:S(2)}) collective-permute-start(bf16[1,96,1024]{2,1,0:T(8,128)(2,1)S(1)} %get-tuple-element.4), channel_id=1, source_target_pairs={{0,2},{1,3},{2,0},{3,1},{4,6},{5,7},{6,4},{7,5},{8,10},{9,11},{10,... | collective-permute-start | bytes 589832 | tf_op jit(solution)/shard_map/ppermute | solution.py:21
  85.4 23.3 %collective-permute-start.2 = (bf16[1,96,1024]{2,1,0:T(8,128)(2,1)S(1)}, bf16[1,96,1024]{2,1,0:T(8,128)(2,1)S(1)}, u32[]{:S(2)}, u32[]{:S(2)}) collective-permute-start(bf16[1,96,1024]{2,1,0:T(8,128)(2,1)S(1)} %get-tuple-element.3), channel_id=1, source_target_pairs={{0,3},{1,2},{2,1},{3,0},{4,7},{5,6},{6,5},{7,4},{8,11},{9,10},{10,... | collective-permute-start | bytes 589832 | tf_op jit(solution)/shard_map/ppermute | solution.py:21
Sparse Core Ops, SparseCore 0:
  9.9 31.5 all-gather.2
  69.3 37.4 reduce-scatter.1
